TPU v7x, 32 devices: a whole 2x2x4 slice. The times are simulated.
32 devices in a mesh: gx: 4 (over y, x), gy: 8 (over z, core).
Axes of the slice: x: 2, y: 2, z: 4, core: 2. Of those that a mesh axis runs over, the one named last changes fastest.
Arguments:
- basis: float32 [4, 8, 3, 32, 192], P('gx', 'gy'), may hold values from -6 to 6
- coupling: bfloat16 [4, 8, 81, 192, 192], P('gx', 'gy'), as said below
- cpl_dst: int32 [4, 8, 81], P('gx', 'gy'), may hold values from 0 to 3, as said below
- cpl_src: int32 [4, 8, 81], P('gx', 'gy'), may hold values from 0 to 26, as said below
Outputs:
- subspace: float32 [4, 8, 3, 32, 192], P('gx', 'gy')
Inputs may be any that keep to these rules, and one draw needn't show every extreme that they name: `cpl_dst`: on each column the live slots come first; a live slot holds its target block's height 0 to 2, every later slot holds 3. The columns at gx index 0 have all 81 slots live. `cpl_src`: A live slot holds (3 dx + dy) * 3 + z for a source block in the column at offsets dx - 1, dy - 1 (periodic) and height z, within one height of the target block, periodically; each source block and column offset appears at most once per target; empty slots hold 0. `coupling`: the assembled matrix is symmetric: for every live slot that couples block i to block j there is a live slot on j's column that couples j to i and holds the transposed block.
All inputs are finite; a program needn't handle non-finite values.
Results may differ from a plain program's by a relative error of at most 0.0085.
Values may be sent and summed in bfloat16 or wider, within the bound.
No kernel may reach another device: no remote copies, remote signals or barrier semaphores. Data moves between devices by JAX's collectives and lax.ppermute only.
A program may use at most 64 MiB of HBM per device.

v0:
```python
import math
import jax
import jax.numpy as jnp
from jax import lax
from jax.sharding import PartitionSpec as P

DEGREE = 8
STEPS = 2
CENTER = 5.0
HALF = 3.0
LOWEST = 0.5


def with_halo(cells, sides, width):
    for axis, dim in sides:
        count = lax.axis_size(axis)
        head = lax.slice_in_dim(cells, 0, width, axis=dim)
        tail = lax.slice_in_dim(cells, cells.shape[dim] - width, cells.shape[dim], axis=dim)
        cells = jnp.concatenate(
            [
                lax.ppermute(tail, axis, [(i, (i + 1) % count) for i in range(count)]),
                cells,
                lax.ppermute(head, axis, [((i + 1) % count, i) for i in range(count)]),
            ],
            axis=dim,
        )
    return cells


def orthonormal(filtered, rows_total):
    local_block = filtered[0, 0]
    partial_gram = jnp.einsum(
        "zvd,zwd->vw", local_block, local_block, precision=lax.Precision.HIGHEST
    )
    gram_matrix = lax.psum(partial_gram, ("gx", "gy"))
    factor = jnp.linalg.cholesky(gram_matrix)
    identity = jnp.eye(local_block.shape[1], dtype=jnp.float32)
    inverse = jax.scipy.linalg.solve_triangular(factor, identity, lower=True)
    result = jnp.einsum("vw,zwd->zvd", inverse, local_block, precision=lax.Precision.HIGHEST)
    return (result * math.sqrt(rows_total))[None, None]


def local(basis, coupling, cpl_dst, cpl_src):
    column_depth = basis.shape[2]
    vector_count = basis.shape[3]
    block_rows = basis.shape[4]
    matrices = coupling[0, 0]
    targets = cpl_dst[0, 0]
    sources = cpl_src[0, 0]
    rows_total = lax.axis_size("gx") * lax.axis_size("gy") * column_depth * block_rows
    select = (targets[None, :] == jnp.arange(column_depth, dtype=jnp.int32)[:, None]).astype(
        jnp.float32
    )

    def apply_operator(current):
        rounded = current.astype(jnp.bfloat16)
        window = with_halo(rounded, (("gx", 0), ("gy", 1)), 1)
        window_cells = window.reshape(9 * column_depth, vector_count, block_rows)
        picked = jnp.take(window_cells, sources, axis=0)
        products = jnp.einsum("kvj,kij->kvi", picked, matrices, preferred_element_type=jnp.float32)
        applied = jnp.einsum("zk,kvi->zvi", select, products, precision=lax.Precision.HIGHEST)
        return applied[None, None]

    sigma_one = HALF / (LOWEST - CENTER)
    current_basis = basis
    for outer in range(STEPS):
        previous = current_basis
        current = sigma_one / HALF * (apply_operator(previous) - CENTER * previous)
        sigma_now = sigma_one
        for inner in range(1, DEGREE):
            sigma_next = 1.0 / (2.0 / sigma_one - sigma_now)
            image = apply_operator(current)
            following = (
                2.0 * sigma_next / HALF * (image - CENTER * current)
                - sigma_now * sigma_next * previous
            )
            previous, current, sigma_now = (current, following, sigma_next)
        current_basis = orthonormal(current, rows_total)
    return current_basis


def solution(mesh):
    placed = (
        P("gx", "gy", None, None, None),
        P("gx", "gy", None, None, None),
        P("gx", "gy", None),
        P("gx", "gy", None),
    )
    return jax.shard_map(
        local,
        mesh=mesh,
        in_specs=placed,
        out_specs=P("gx", "gy", None, None, None),
        check_vma=False,
    )
```

profile of v0, /device:TPU:0, one launch (start us, length us, event | category | flops | bytes accessed | tf_op | source)
XLA Modules:
  0.0 457.4 jit_solution(3541501361220826311)
XLA Ops:
  19.0 5.8 %fusion.30 = f32[81,32,192]{2,1,0:T(8,128)S(1)} fusion(bf16[1,1,81,192,192]{4,3,2,1,0:T(8,128)(2,1)} %param.10, bf16[81,32,192]{2,1,0:T(8,128)(2,1)S(1)} %gather_fusion, pred[81]{0:T(512)(128)(4,1)S(1)} %compare_and_fusion), kind=kOutput, calls=%fused_computation.46 | convolution fusion | flops 191600640 | bytes 8958033 | tf_op jit(solution)/shard_map/kvj,kij->kvi/dot_general | solution.py:60
  33.4 4.6 %collective-permute-done.7 = bf16[3,1,3,32,192]{4,2,3,1,0:T(4,128)(2,1)S(1)} collective-permute-done((bf16[3,1,3,32,192]{4,2,3,1,0:T(4,128)(2,1)S(1)}, bf16[3,1,3,32,192]{4,2,3,1,0:T(4,128)(2,1)S(1)}, u32[]{:S(2)}, u32[]{:S(2)}) %collective-permute-start.7) | collective-permute-done | bytes 110624 | tf_op jit(solution)/shard_map/ppermute | solution.py:23
  41.6 5.8 %fusion.28 = f32[81,32,192]{2,1,0:T(8,128)S(1)} fusion(bf16[1,1,81,192,192]{4,3,2,1,0:T(8,128)(2,1)} %param.10, bf16[81,32,192]{2,1,0:T(8,128)(2,1)S(1)} %gather_fusion.1, pred[81]{0:T(512)(128)(4,1)S(1)} %compare_and_fusion), kind=kOutput, calls=%fused_computation.44 | convolution fusion | flops 191600640 | bytes 8958033 | tf_op jit(solution)/shard_map/kvj,kij->kvi/dot_general | solution.py:60
  66.1 5.8 %fusion.26 = f32[81,32,192]{2,1,0:T(8,128)S(1)} fusion(bf16[1,1,81,192,192]{4,3,2,1,0:T(8,128)(2,1)} %param.10, bf16[81,32,192]{2,1,0:T(8,128)(2,1)S(1)} %gather_fusion.2, pred[81]{0:T(512)(128)(4,1)S(1)} %compare_and_fusion), kind=kOutput, calls=%fused_computation.42 | convolution fusion | flops 191600640 | bytes 8958033 | tf_op jit(solution)/shard_map/kvj,kij->kvi/dot_general | solution.py:60
  81.3 4.6 %collective-permute-done.15 = bf16[3,1,3,32,192]{4,2,3,1,0:T(4,128)(2,1)S(1)} collective-permute-done((bf16[3,1,3,32,192]{4,2,3,1,0:T(4,128)(2,1)S(1)}, bf16[3,1,3,32,192]{4,2,3,1,0:T(4,128)(2,1)S(1)}, u32[]{:S(2)}, u32[]{:S(2)}) %collective-permute-start.15) | collective-permute-done | bytes 110624 | tf_op jit(solution)/shard_map/ppermute | solution.py:23
  89.1 5.8 %fusion.24 = f32[81,32,192]{2,1,0:T(8,128)S(1)} fusion(bf16[1,1,81,192,192]{4,3,2,1,0:T(8,128)(2,1)} %param.10, bf16[81,32,192]{2,1,0:T(8,128)(2,1)S(1)} %gather_fusion.3, pred[81]{0:T(512)(128)(4,1)S(1)} %compare_and_fusion), kind=kOutput, calls=%fused_computation.40 | convolution fusion | flops 191600640 | bytes 8958033 | tf_op jit(solution)/shard_map/kvj,kij->kvi/dot_general | solution.py:60
  104.5 4.8 %collective-permute-done.19 = bf16[3,1,3,32,192]{4,2,3,1,0:T(4,128)(2,1)S(1)} collective-permute-done((bf16[3,1,3,32,192]{4,2,3,1,0:T(4,128)(2,1)S(1)}, bf16[3,1,3,32,192]{4,2,3,1,0:T(4,128)(2,1)S(1)}, u32[]{:S(2)}, u32[]{:S(2)}) %collective-permute-start.19) | collective-permute-done | bytes 110624 | tf_op jit(solution)/shard_map/ppermute | solution.py:23
  112.7 5.8 %fusion.22 = f32[81,32,192]{2,1,0:T(8,128)S(1)} fusion(bf16[1,1,81,192,192]{4,3,2,1,0:T(8,128)(2,1)} %param.10, bf16[81,32,192]{2,1,0:T(8,128)(2,1)S(1)} %gather_fusion.4, pred[81]{0:T(512)(128)(4,1)S(1)} %compare_and_fusion), kind=kOutput, calls=%fused_computation.38 | convolution fusion | flops 191600640 | bytes 8958033 | tf_op jit(solution)/shard_map/kvj,kij->kvi/dot_general | solution.py:60
  127.5 4.6 %collective-permute-done.23 = bf16[3,1,3,32,192]{4,2,3,1,0:T(4,128)(2,1)S(1)} collective-permute-done((bf16[3,1,3,32,192]{4,2,3,1,0:T(4,128)(2,1)S(1)}, bf16[3,1,3,32,192]{4,2,3,1,0:T(4,128)(2,1)S(1)}, u32[]{:S(2)}, u32[]{:S(2)}) %collective-permute-start.23) | collective-permute-done | bytes 110624 | tf_op jit(solution)/shard_map/ppermute | solution.py:23
  135.3 5.8 %fusion.20 = f32[81,32,192]{2,1,0:T(8,128)S(1)} fusion(bf16[1,1,81,192,192]{4,3,2,1,0:T(8,128)(2,1)} %param.10, bf16[81,32,192]{2,1,0:T(8,128)(2,1)S(1)} %gather_fusion.5, pred[81]{0:T(512)(128)(4,1)S(1)} %compare_and_fusion), kind=kOutput, calls=%fused_computation.36 | convolution fusion | flops 191600640 | bytes 8958033 | tf_op jit(solution)/shard_map/kvj,kij->kvi/dot_general | solution.py:60
  150.9 4.6 %collective-permute-done.27 = bf16[3,1,3,32,192]{4,2,3,1,0:T(4,128)(2,1)S(1)} collective-permute-done((bf16[3,1,3,32,192]{4,2,3,1,0:T(4,128)(2,1)S(1)}, bf16[3,1,3,32,192]{4,2,3,1,0:T(4,128)(2,1)S(1)}, u32[]{:S(2)}, u32[]{:S(2)}) %collective-permute-start.27) | collective-permute-done | bytes 110624 | tf_op jit(solution)/shard_map/ppermute | solution.py:23
  159.1 5.8 %fusion.18 = f32[81,32,192]{2,1,0:T(8,128)S(1)} fusion(bf16[1,1,81,192,192]{4,3,2,1,0:T(8,128)(2,1)} %param.10, bf16[81,32,192]{2,1,0:T(8,128)(2,1)S(1)} %gather_fusion.6, pred[81]{0:T(512)(128)(4,1)S(1)} %compare_and_fusion), kind=kOutput, calls=%fused_computation.34 | convolution fusion | flops 191600640 | bytes 8958033 | tf_op jit(solution)/shard_map/kvj,kij->kvi/dot_general | solution.py:60
  174.5 4.6 %collective-permute-done.31 = bf16[3,1,3,32,192]{4,2,3,1,0:T(4,128)(2,1)S(1)} collective-permute-done((bf16[3,1,3,32,192]{4,2,3,1,0:T(4,128)(2,1)S(1)}, bf16[3,1,3,32,192]{4,2,3,1,0:T(4,128)(2,1)S(1)}, u32[]{:S(2)}, u32[]{:S(2)}) %collective-permute-start.31) | collective-permute-done | bytes 110624 | tf_op jit(solution)/shard_map/ppermute | solution.py:23
  182.4 5.8 %fusion.16 = f32[81,32,192]{2,1,0:T(8,128)S(1)} fusion(bf16[1,1,81,192,192]{4,3,2,1,0:T(8,128)(2,1)} %param.10, bf16[81,32,192]{2,1,0:T(8,128)(2,1)S(1)} %gather_fusion.7, pred[81]{0:T(512)(128)(4,1)S(1)} %compare_and_fusion), kind=kOutput, calls=%fused_computation.32 | convolution fusion | flops 191600640 | bytes 8958033 | tf_op jit(solution)/shard_map/kvj,kij->kvi/dot_general | solution.py:60
  191.0 38.2 %psum.14 = f32[32,32]{0,1:T(8,128)S(1)} all-reduce(f32[32,32]{0,1:T(8,128)S(1)} %convolution_bitcast_fusion.3), channel_id=1, replica_groups=mesh['gx'=4,'gy'=8] {'gx','gy'}, use_global_device_ids=true, to_apply=%region_0.0 | all-reduce | flops 1024 | bytes 8192 | tf_op jit(solution)/shard_map/psum | solution.py:35
  251.2 5.8 %fusion.14 = f32[81,32,192]{2,1,0:T(8,128)S(1)} fusion(bf16[1,1,81,192,192]{4,3,2,1,0:T(8,128)(2,1)} %param.10, bf16[81,32,192]{2,1,0:T(8,128)(2,1)S(1)} %gather_fusion.8, pred[81]{0:T(512)(128)(4,1)S(1)} %compare_and_fusion), kind=kOutput, calls=%fused_computation.30 | convolution fusion | flops 191600640 | bytes 8958033 | tf_op jit(solution)/shard_map/kvj,kij->kvi/dot_general | solution.py:60
  272.5 5.8 %fusion.12 = f32[81,32,192]{2,1,0:T(8,128)S(1)} fusion(bf16[1,1,81,192,192]{4,3,2,1,0:T(8,128)(2,1)} %param.10, bf16[81,32,192]{2,1,0:T(8,128)(2,1)S(1)} %gather_fusion.9, pred[81]{0:T(512)(128)(4,1)S(1)} %compare_and_fusion), kind=kOutput, calls=%fused_computation.28 | convolution fusion | flops 191600640 | bytes 8958033 | tf_op jit(solution)/shard_map/kvj,kij->kvi/dot_general | solution.py:60
  295.0 5.8 %fusion.10 = f32[81,32,192]{2,1,0:T(8,128)S(1)} fusion(bf16[1,1,81,192,192]{4,3,2,1,0:T(8,128)(2,1)} %param.10, bf16[81,32,192]{2,1,0:T(8,128)(2,1)S(1)} %gather_fusion.10, pred[81]{0:T(512)(128)(4,1)S(1)} %compare_and_fusion), kind=kOutput, calls=%fused_computation.26 | convolution fusion | flops 191600640 | bytes 8958033 | tf_op jit(solution)/shard_map/kvj,kij->kvi/dot_general | solution.py:60
  316.3 5.8 %fusion.8 = f32[81,32,192]{2,1,0:T(8,128)S(1)} fusion(bf16[1,1,81,192,192]{4,3,2,1,0:T(8,128)(2,1)} %param.10, bf16[81,32,192]{2,1,0:T(8,128)(2,1)S(1)} %gather_fusion.11, pred[81]{0:T(512)(128)(4,1)S(1)} %compare_and_fusion), kind=kOutput, calls=%fused_computation.24 | convolution fusion | flops 191600640 | bytes 8958033 | tf_op jit(solution)/shard_map/kvj,kij->kvi/dot_general | solution.py:60
  338.0 5.8 %fusion.6 = f32[81,32,192]{2,1,0:T(8,128)S(1)} fusion(bf16[1,1,81,192,192]{4,3,2,1,0:T(8,128)(2,1)} %param.10, bf16[81,32,192]{2,1,0:T(8,128)(2,1)S(1)} %gather_fusion.12, pred[81]{0:T(512)(128)(4,1)S(1)} %compare_and_fusion), kind=kOutput, calls=%fused_computation.22 | convolution fusion | flops 191600640 | bytes 8958033 | tf_op jit(solution)/shard_map/kvj,kij->kvi/dot_general | solution.py:60
  359.8 5.8 %fusion.4 = f32[81,32,192]{2,1,0:T(8,128)S(1)} fusion(bf16[1,1,81,192,192]{4,3,2,1,0:T(8,128)(2,1)} %param.10, bf16[81,32,192]{2,1,0:T(8,128)(2,1)S(1)} %gather_fusion.13, pred[81]{0:T(512)(128)(4,1)S(1)} %compare_and_fusion), kind=kOutput, calls=%fused_computation.20 | convolution fusion | flops 191600640 | bytes 8958033 | tf_op jit(solution)/shard_map/kvj,kij->kvi/dot_general | solution.py:60
  381.7 5.8 %fusion.2 = f32[81,32,192]{2,1,0:T(8,128)S(1)} fusion(bf16[1,1,81,192,192]{4,3,2,1,0:T(8,128)(2,1)} %param.10, bf16[81,32,192]{2,1,0:T(8,128)(2,1)S(1)} %gather_fusion.14, pred[81]{0:T(512)(128)(4,1)S(1)} %compare_and_fusion), kind=kOutput, calls=%fused_computation.18 | convolution fusion | flops 191600640 | bytes 8958033 | tf_op jit(solution)/shard_map/kvj,kij->kvi/dot_general | solution.py:60
  403.0 5.8 %fusion = f32[81,32,192]{2,1,0:T(8,128)S(1)} fusion(bf16[1,1,81,192,192]{4,3,2,1,0:T(8,128)(2,1)} %param.10, bf16[81,32,192]{2,1,0:T(8,128)(2,1)S(1)} %gather_fusion.15, pred[81]{0:T(512)(128)(4,1)S(1)} %compare_and_fusion), kind=kOutput, calls=%fused_computation.16 | convolution fusion | flops 191600640 | bytes 8958033 | tf_op jit(solution)/shard_map/kvj,kij->kvi/dot_general | solution.py:60
  411.6 37.7 %psum.15 = f32[32,32]{0,1:T(8,128)S(1)} all-reduce(f32[32,32]{0,1:T(8,128)S(1)} %convolution_bitcast_fusion.1), channel_id=1, replica_groups=mesh['gx'=4,'gy'=8] {'gx','gy'}, use_global_device_ids=true, to_apply=%region_3.7 | all-reduce | flops 1024 | bytes 8192 | tf_op jit(solution)/shard_map/psum | solution.py:35
  (230 shorter events, 260.0 us)
Async XLA Ops:
  0.9 5.6 %collective-permute-start.1 = (bf16[1,1,3,32,192]{4,3,2,1,0:T(8,128)(2,1)S(1)}, bf16[1,1,3,32,192]{4,3,2,1,0:T(8,128)(2,1)S(1)}, u32[]{:S(2)}, u32[]{:S(2)}) collective-permute-start(bf16[1,1,3,32,192]{4,3,2,1,0:T(8,128)(2,1)S(1)} %convert_element_type.82), channel_id=1, source_target_pairs={{8,0},{16,8},{24,16},{0,24},{9,1},{17,9},{25,17},{1,25},{10,2},{18... | collective-permute-start | bytes 110600 | tf_op jit(solution)/shard_map/ppermute | solution.py:23
  9.8 5.4 %collective-permute-start.3 = (bf16[3,1,3,32,192]{4,3,2,1,0:T(8,128)(2,1)S(1)}, bf16[3,1,3,32,192]{4,3,2,1,0:T(8,128)(2,1)S(1)}, u32[]{:S(2)}, u32[]{:S(2)}) collective-permute-start(bf16[3,1,3,32,192]{4,3,2,1,0:T(8,128)(2,1)S(1)} %pad_maximum_fusion.23), channel_id=1, source_target_pairs={{1,0},{2,1},{3,2},{4,3},{5,4},{6,5},{7,6},{0,7},{9,8},{10,9},{11,1... | collective-permute-start | bytes 331784 | tf_op jit(solution)/shard_map/ppermute | solution.py:23
  11.5 6.7 %collective-permute-start.2 = (bf16[3,1,3,32,192]{4,3,2,1,0:T(8,128)(2,1)S(1)}, bf16[3,1,3,32,192]{4,3,2,1,0:T(8,128)(2,1)S(1)}, u32[]{:S(2)}, u32[]{:S(2)}) collective-permute-start(bf16[3,1,3,32,192]{4,3,2,1,0:T(8,128)(2,1)S(1)} %pad_maximum_fusion.23), channel_id=1, source_target_pairs={{0,1},{1,2},{2,3},{3,4},{4,5},{5,6},{6,7},{7,0},{8,9},{9,10},{10,1... | collective-permute-start | bytes 331784 | tf_op jit(solution)/shard_map/ppermute | solution.py:21
  27.5 5.2 %collective-permute-start.4 = (bf16[1,1,3,32,192]{4,2,3,1,0:T(4,128)(2,1)S(1)}, bf16[1,1,3,32,192]{4,2,3,1,0:T(4,128)(2,1)S(1)}, u32[]{:S(2)}, u32[]{:S(2)}) collective-permute-start(bf16[1,1,3,32,192]{4,2,3,1,0:T(4,128)(2,1)S(1)} %get-tuple-element.18), channel_id=1, source_target_pairs={{0,8},{8,16},{16,24},{24,0},{1,9},{9,17},{17,25},{25,1},{2,10},{10... | collective-permute-start | bytes 110600 | tf_op jit(solution)/shard_map/ppermute | solution.py:21
  32.9 7.3 %collective-permute-start.6 = (bf16[3,1,3,32,192]{4,2,3,1,0:T(4,128)(2,1)S(1)}, bf16[3,1,3,32,192]{4,2,3,1,0:T(4,128)(2,1)S(1)}, u32[]{:S(2)}, u32[]{:S(2)}) collective-permute-start(bf16[3,1,3,32,192]{4,2,3,1,0:T(4,128)(2,1)S(1)} %pad_maximum_fusion.16), channel_id=1, source_target_pairs={{0,1},{1,2},{2,3},{3,4},{4,5},{5,6},{6,7},{7,0},{8,9},{9,10},{10,1... | collective-permute-start | bytes 331784 | tf_op jit(solution)/shard_map/ppermute | solution.py:21
  56.3 5.3 %collective-permute-start.11 = (bf16[3,1,3,32,192]{4,2,3,1,0:T(4,128)(2,1)S(1)}, bf16[3,1,3,32,192]{4,2,3,1,0:T(4,128)(2,1)S(1)}, u32[]{:S(2)}, u32[]{:S(2)}) collective-permute-start(bf16[3,1,3,32,192]{4,2,3,1,0:T(4,128)(2,1)S(1)} %pad_maximum_fusion.17), channel_id=1, source_target_pairs={{1,0},{2,1},{3,2},{4,3},{5,4},{6,5},{7,6},{0,7},{9,8},{10,9},{11,1... | collective-permute-start | bytes 331784 | tf_op jit(solution)/shard_map/ppermute | solution.py:23
  57.7 7.0 %collective-permute-start.10 = (bf16[3,1,3,32,192]{4,2,3,1,0:T(4,128)(2,1)S(1)}, bf16[3,1,3,32,192]{4,2,3,1,0:T(4,128)(2,1)S(1)}, u32[]{:S(2)}, u32[]{:S(2)}) collective-permute-start(bf16[3,1,3,32,192]{4,2,3,1,0:T(4,128)(2,1)S(1)} %pad_maximum_fusion.17), channel_id=1, source_target_pairs={{0,1},{1,2},{2,3},{3,4},{4,5},{5,6},{6,7},{7,0},{8,9},{9,10},{10,1... | collective-permute-start | bytes 331784 | tf_op jit(solution)/shard_map/ppermute | solution.py:21
  80.8 5.2 %collective-permute-start.15 = (bf16[3,1,3,32,192]{4,2,3,1,0:T(4,128)(2,1)S(1)}, bf16[3,1,3,32,192]{4,2,3,1,0:T(4,128)(2,1)S(1)}, u32[]{:S(2)}, u32[]{:S(2)}) collective-permute-start(bf16[3,1,3,32,192]{4,2,3,1,0:T(4,128)(2,1)S(1)} %pad_maximum_fusion.18), channel_id=1, source_target_pairs={{1,0},{2,1},{3,2},{4,3},{5,4},{6,5},{7,6},{0,7},{9,8},{10,9},{11,1... | collective-permute-start | bytes 331784 | tf_op jit(solution)/shard_map/ppermute | solution.py:23
  80.8 6.9 %collective-permute-start.14 = (bf16[3,1,3,32,192]{4,2,3,1,0:T(4,128)(2,1)S(1)}, bf16[3,1,3,32,192]{4,2,3,1,0:T(4,128)(2,1)S(1)}, u32[]{:S(2)}, u32[]{:S(2)}) collective-permute-start(bf16[3,1,3,32,192]{4,2,3,1,0:T(4,128)(2,1)S(1)} %pad_maximum_fusion.18), channel_id=1, source_target_pairs={{0,1},{1,2},{2,3},{3,4},{4,5},{5,6},{6,7},{7,0},{8,9},{9,10},{10,1... | collective-permute-start | bytes 331784 | tf_op jit(solution)/shard_map/ppermute | solution.py:21
  103.8 5.5 %collective-permute-start.19 = (bf16[3,1,3,32,192]{4,2,3,1,0:T(4,128)(2,1)S(1)}, bf16[3,1,3,32,192]{4,2,3,1,0:T(4,128)(2,1)S(1)}, u32[]{:S(2)}, u32[]{:S(2)}) collective-permute-start(bf16[3,1,3,32,192]{4,2,3,1,0:T(4,128)(2,1)S(1)} %pad_maximum_fusion.19), channel_id=1, source_target_pairs={{1,0},{2,1},{3,2},{4,3},{5,4},{6,5},{7,6},{0,7},{9,8},{10,9},{11,1... | collective-permute-start | bytes 331784 | tf_op jit(solution)/shard_map/ppermute | solution.py:23
  104.2 7.1 %collective-permute-start.18 = (bf16[3,1,3,32,192]{4,2,3,1,0:T(4,128)(2,1)S(1)}, bf16[3,1,3,32,192]{4,2,3,1,0:T(4,128)(2,1)S(1)}, u32[]{:S(2)}, u32[]{:S(2)}) collective-permute-start(bf16[3,1,3,32,192]{4,2,3,1,0:T(4,128)(2,1)S(1)} %pad_maximum_fusion.19), channel_id=1, source_target_pairs={{0,1},{1,2},{2,3},{3,4},{4,5},{5,6},{6,7},{7,0},{8,9},{9,10},{10,1... | collective-permute-start | bytes 331784 | tf_op jit(solution)/shard_map/ppermute | solution.py:21
  127.0 5.2 %collective-permute-start.23 = (bf16[3,1,3,32,192]{4,2,3,1,0:T(4,128)(2,1)S(1)}, bf16[3,1,3,32,192]{4,2,3,1,0:T(4,128)(2,1)S(1)}, u32[]{:S(2)}, u32[]{:S(2)}) collective-permute-start(bf16[3,1,3,32,192]{4,2,3,1,0:T(4,128)(2,1)S(1)} %pad_maximum_fusion.20), channel_id=1, source_target_pairs={{1,0},{2,1},{3,2},{4,3},{5,4},{6,5},{7,6},{0,7},{9,8},{10,9},{11,1... | collective-permute-start | bytes 331784 | tf_op jit(solution)/shard_map/ppermute | solution.py:23
  127.0 6.9 %collective-permute-start.22 = (bf16[3,1,3,32,192]{4,2,3,1,0:T(4,128)(2,1)S(1)}, bf16[3,1,3,32,192]{4,2,3,1,0:T(4,128)(2,1)S(1)}, u32[]{:S(2)}, u32[]{:S(2)}) collective-permute-start(bf16[3,1,3,32,192]{4,2,3,1,0:T(4,128)(2,1)S(1)} %pad_maximum_fusion.20), channel_id=1, source_target_pairs={{0,1},{1,2},{2,3},{3,4},{4,5},{5,6},{6,7},{7,0},{8,9},{9,10},{10,1... | collective-permute-start | bytes 331784 | tf_op jit(solution)/shard_map/ppermute | solution.py:21
  150.0 5.6 %collective-permute-start.27 = (bf16[3,1,3,32,192]{4,2,3,1,0:T(4,128)(2,1)S(1)}, bf16[3,1,3,32,192]{4,2,3,1,0:T(4,128)(2,1)S(1)}, u32[]{:S(2)}, u32[]{:S(2)}) collective-permute-start(bf16[3,1,3,32,192]{4,2,3,1,0:T(4,128)(2,1)S(1)} %pad_maximum_fusion.21), channel_id=1, source_target_pairs={{1,0},{2,1},{3,2},{4,3},{5,4},{6,5},{7,6},{0,7},{9,8},{10,9},{11,1... | collective-permute-start | bytes 331784 | tf_op jit(solution)/shard_map/ppermute | solution.py:23
  150.5 7.3 %collective-permute-start.26 = (bf16[3,1,3,32,192]{4,2,3,1,0:T(4,128)(2,1)S(1)}, bf16[3,1,3,32,192]{4,2,3,1,0:T(4,128)(2,1)S(1)}, u32[]{:S(2)}, u32[]{:S(2)}) collective-permute-start(bf16[3,1,3,32,192]{4,2,3,1,0:T(4,128)(2,1)S(1)} %pad_maximum_fusion.21), channel_id=1, source_target_pairs={{0,1},{1,2},{2,3},{3,4},{4,5},{5,6},{6,7},{7,0},{8,9},{9,10},{10,1... | collective-permute-start | bytes 331784 | tf_op jit(solution)/shard_map/ppermute | solution.py:21
  174.2 6.9 %collective-permute-start.30 = (bf16[3,1,3,32,192]{4,2,3,1,0:T(4,128)(2,1)S(1)}, bf16[3,1,3,32,192]{4,2,3,1,0:T(4,128)(2,1)S(1)}, u32[]{:S(2)}, u32[]{:S(2)}) collective-permute-start(bf16[3,1,3,32,192]{4,2,3,1,0:T(4,128)(2,1)S(1)} %pad_maximum_fusion.22), channel_id=1, source_target_pairs={{0,1},{1,2},{2,3},{3,4},{4,5},{5,6},{6,7},{7,0},{8,9},{9,10},{10,1... | collective-permute-start | bytes 331784 | tf_op jit(solution)/shard_map/ppermute | solution.py:21
  243.9 6.5 %collective-permute-start.34 = (bf16[3,1,3,32,192]{4,3,2,1,0:T(8,128)(2,1)S(1)}, bf16[3,1,3,32,192]{4,3,2,1,0:T(8,128)(2,1)S(1)}, u32[]{:S(2)}, u32[]{:S(2)}) collective-permute-start(bf16[3,1,3,32,192]{4,3,2,1,0:T(8,128)(2,1)S(1)} %pad_maximum_fusion.24), channel_id=1, source_target_pairs={{0,1},{1,2},{2,3},{3,4},{4,5},{5,6},{6,7},{7,0},{8,9},{9,10},{10,1... | collective-permute-start | bytes 331784 | tf_op jit(solution)/shard_map/ppermute | solution.py:21
  265.3 6.4 %collective-permute-start.38 = (bf16[3,1,3,32,192]{4,3,2,1,0:T(8,128)(2,1)S(1)}, bf16[3,1,3,32,192]{4,3,2,1,0:T(8,128)(2,1)S(1)}, u32[]{:S(2)}, u32[]{:S(2)}) collective-permute-start(bf16[3,1,3,32,192]{4,3,2,1,0:T(8,128)(2,1)S(1)} %pad_maximum_fusion.25), channel_id=1, source_target_pairs={{0,1},{1,2},{2,3},{3,4},{4,5},{5,6},{6,7},{7,0},{8,9},{9,10},{10,1... | collective-permute-start | bytes 331784 | tf_op jit(solution)/shard_map/ppermute | solution.py:21
  287.6 6.6 %collective-permute-start.42 = (bf16[3,1,3,32,192]{4,3,2,1,0:T(8,128)(2,1)S(1)}, bf16[3,1,3,32,192]{4,3,2,1,0:T(8,128)(2,1)S(1)}, u32[]{:S(2)}, u32[]{:S(2)}) collective-permute-start(bf16[3,1,3,32,192]{4,3,2,1,0:T(8,128)(2,1)S(1)} %pad_maximum_fusion.26), channel_id=1, source_target_pairs={{0,1},{1,2},{2,3},{3,4},{4,5},{5,6},{6,7},{7,0},{8,9},{9,10},{10,1... | collective-permute-start | bytes 331784 | tf_op jit(solution)/shard_map/ppermute | solution.py:21
  309.1 6.4 %collective-permute-start.46 = (bf16[3,1,3,32,192]{4,3,2,1,0:T(8,128)(2,1)S(1)}, bf16[3,1,3,32,192]{4,3,2,1,0:T(8,128)(2,1)S(1)}, u32[]{:S(2)}, u32[]{:S(2)}) collective-permute-start(bf16[3,1,3,32,192]{4,3,2,1,0:T(8,128)(2,1)S(1)} %pad_maximum_fusion.27), channel_id=1, source_target_pairs={{0,1},{1,2},{2,3},{3,4},{4,5},{5,6},{6,7},{7,0},{8,9},{9,10},{10,1... | collective-permute-start | bytes 331784 | tf_op jit(solution)/shard_map/ppermute | solution.py:21
  330.4 6.8 %collective-permute-start.50 = (bf16[3,1,3,32,192]{4,3,2,1,0:T(8,128)(2,1)S(1)}, bf16[3,1,3,32,192]{4,3,2,1,0:T(8,128)(2,1)S(1)}, u32[]{:S(2)}, u32[]{:S(2)}) collective-permute-start(bf16[3,1,3,32,192]{4,3,2,1,0:T(8,128)(2,1)S(1)} %pad_maximum_fusion.28), channel_id=1, source_target_pairs={{0,1},{1,2},{2,3},{3,4},{4,5},{5,6},{6,7},{7,0},{8,9},{9,10},{10,1... | collective-permute-start | bytes 331784 | tf_op jit(solution)/shard_map/ppermute | solution.py:21
  352.6 6.4 %collective-permute-start.54 = (bf16[3,1,3,32,192]{4,3,2,1,0:T(8,128)(2,1)S(1)}, bf16[3,1,3,32,192]{4,3,2,1,0:T(8,128)(2,1)S(1)}, u32[]{:S(2)}, u32[]{:S(2)}) collective-permute-start(bf16[3,1,3,32,192]{4,3,2,1,0:T(8,128)(2,1)S(1)} %pad_maximum_fusion.29), channel_id=1, source_target_pairs={{0,1},{1,2},{2,3},{3,4},{4,5},{5,6},{6,7},{7,0},{8,9},{9,10},{10,1... | collective-permute-start | bytes 331784 | tf_op jit(solution)/shard_map/ppermute | solution.py:21
  374.3 6.6 %collective-permute-start.58 = (bf16[3,1,3,32,192]{4,3,2,1,0:T(8,128)(2,1)S(1)}, bf16[3,1,3,32,192]{4,3,2,1,0:T(8,128)(2,1)S(1)}, u32[]{:S(2)}, u32[]{:S(2)}) collective-permute-start(bf16[3,1,3,32,192]{4,3,2,1,0:T(8,128)(2,1)S(1)} %pad_maximum_fusion.30), channel_id=1, source_target_pairs={{0,1},{1,2},{2,3},{3,4},{4,5},{5,6},{6,7},{7,0},{8,9},{9,10},{10,1... | collective-permute-start | bytes 331784 | tf_op jit(solution)/shard_map/ppermute | solution.py:21
  395.8 6.4 %collective-permute-start.62 = (bf16[3,1,3,32,192]{4,3,2,1,0:T(8,128)(2,1)S(1)}, bf16[3,1,3,32,192]{4,3,2,1,0:T(8,128)(2,1)S(1)}, u32[]{:S(2)}, u32[]{:S(2)}) collective-permute-start(bf16[3,1,3,32,192]{4,3,2,1,0:T(8,128)(2,1)S(1)} %pad_maximum_fusion.31), channel_id=1, source_target_pairs={{0,1},{1,2},{2,3},{3,4},{4,5},{5,6},{6,7},{7,0},{8,9},{9,10},{10,1... | collective-permute-start | bytes 331784 | tf_op jit(solution)/shard_map/ppermute | solution.py:21
  (42 other events, 194.2 us)
where the time goes:
time: 466 us; the launch traced here: 457 us
  waiting for transfers between devices  164 us (35%)
  matrix products  136 us (29%)
  blocking collectives  75.9 us (16%)
  starting transfers between devices  47.7 us (10%)
  other arithmetic  22.3 us (5%)
  local copies, waits for them, and re-layouts  11.6 us (2%)
    ppermute x32, waiting for transfers between devices, with_halo(): lax.ppermute(head, axis, [((i + 1) % count, i) for i in range(count)])  95.2 us
    dot_general x16, matrix products, apply_operator(): jnp.einsum('kvj,kij->kvi', picked, matrices, preferred_element_type=jnp.f...  92.9 us
    psum x2, blocking collectives, orthonormal(): gram_matrix = lax.psum(partial_gram, ('gx', 'gy'))  75.9 us
    ppermute x32, waiting for transfers between devices, with_halo(): lax.ppermute(tail, axis, [(i, (i + 1) % count) for i in range(count)])  68.3 us
    dot_general x16, matrix products, apply_operator(): jnp.einsum('zk,kvi->zvi', select, products, precision=lax.Precision.HIGHEST)  40.6 us
    ppermute x32, starting transfers between devices, with_halo(): lax.ppermute(tail, axis, [(i, (i + 1) % count) for i in range(count)])  24.6 us
    ppermute x32, starting transfers between devices, with_halo(): lax.ppermute(head, axis, [((i + 1) % count, i) for i in range(count)])  23.1 us
    gather x16, local copies, waits for them, and re-layouts, apply_operator(): picked = jnp.take(window_cells, sources, axis=0)  10.9 us
  transfers between devices with their start and end apart: 64, of which 64 were waited for; matrix products, arithmetic and copies ran while one was open for 0% of the time, Pallas kernels for 0%

commit v1 on v0

--- a/solution.py
+++ b/solution.py
@@ -32,7 +32,7 @@
     partial_gram = jnp.einsum(
         "zvd,zwd->vw", local_block, local_block, precision=lax.Precision.HIGHEST
     )
-    gram_matrix = lax.psum(partial_gram, ("gx", "gy"))
+    gram_matrix = lax.psum(lax.psum(partial_gram, "gy"), "gx")
     factor = jnp.linalg.cholesky(gram_matrix)
     identity = jnp.eye(local_block.shape[1], dtype=jnp.float32)
     inverse = jax.scipy.linalg.solve_triangular(factor, identity, lower=True)

time: 466 us -> 472 us (1.013)
  blocking collectives: 75.9 us -> 84 us
    psum x2 -> x4, blocking collectives: 75.9 us -> 84 us  [orthonormal(): gram_matrix = lax.psum(lax.psum(partial_gram, 'gy'), 'gx')]
where the time goes in v1:
time: 472 us; the launch traced here: 464 us
  waiting for transfers between devices  162 us (34%)
  matrix products  136 us (29%)
  blocking collectives  84 us (18%)
  starting transfers between devices  47.4 us (10%)
  other arithmetic  22.3 us (5%)
  local copies, waits for them, and re-layouts  11.6 us (2%)
    ppermute x32, waiting for transfers between devices, with_halo(): lax.ppermute(head, axis, [((i + 1) % count, i) for i in range(count)])  95.9 us
    dot_general x16, matrix products, apply_operator(): jnp.einsum('kvj,kij->kvi', picked, matrices, preferred_element_type=jnp.f...  92.9 us
    psum x4, blocking collectives, orthonormal(): gram_matrix = lax.psum(lax.psum(partial_gram, 'gy'), 'gx')  84 us
    ppermute x32, waiting for transfers between devices, with_halo(): lax.ppermute(tail, axis, [(i, (i + 1) % count) for i in range(count)])  66.2 us
    dot_general x16, matrix products, apply_operator(): jnp.einsum('zk,kvi->zvi', select, products, precision=lax.Precision.HIGHEST)  40.6 us
    ppermute x32, starting transfers between devices, with_halo(): lax.ppermute(tail, axis, [(i, (i + 1) % count) for i in range(count)])  25.9 us
    ppermute x32, starting transfers between devices, with_halo(): lax.ppermute(head, axis, [((i + 1) % count, i) for i in range(count)])  21.5 us
    gather x16, local copies, waits for them, and re-layouts, apply_operator(): picked = jnp.take(window_cells, sources, axis=0)  10.9 us
  transfers between devices with their start and end apart: 64, of which 64 were waited for; matrix products, arithmetic and copies ran while one was open for 0% of the time, Pallas kernels for 0%

profile of v1, /device:TPU:0, one launch (start us, length us, event | category | flops | bytes accessed | tf_op | source)
XLA Modules:
  0.0 463.7 jit_solution(6448188568971137154)
XLA Ops:
  19.0 5.8 %fusion.30 = f32[81,32,192]{2,1,0:T(8,128)S(1)} fusion(bf16[1,1,81,192,192]{4,3,2,1,0:T(8,128)(2,1)} %param.10, bf16[81,32,192]{2,1,0:T(8,128)(2,1)S(1)} %gather_fusion, pred[81]{0:T(512)(128)(4,1)S(1)} %compare_and_fusion), kind=kOutput, calls=%fused_computation.46 | convolution fusion | flops 191600640 | bytes 8958033 | tf_op jit(solution)/shard_map/kvj,kij->kvi/dot_general | solution.py:60
  41.6 5.8 %fusion.28 = f32[81,32,192]{2,1,0:T(8,128)S(1)} fusion(bf16[1,1,81,192,192]{4,3,2,1,0:T(8,128)(2,1)} %param.10, bf16[81,32,192]{2,1,0:T(8,128)(2,1)S(1)} %gather_fusion.1, pred[81]{0:T(512)(128)(4,1)S(1)} %compare_and_fusion), kind=kOutput, calls=%fused_computation.44 | convolution fusion | flops 191600640 | bytes 8958033 | tf_op jit(solution)/shard_map/kvj,kij->kvi/dot_general | solution.py:60
  66.1 5.8 %fusion.26 = f32[81,32,192]{2,1,0:T(8,128)S(1)} fusion(bf16[1,1,81,192,192]{4,3,2,1,0:T(8,128)(2,1)} %param.10, bf16[81,32,192]{2,1,0:T(8,128)(2,1)S(1)} %gather_fusion.2, pred[81]{0:T(512)(128)(4,1)S(1)} %compare_and_fusion), kind=kOutput, calls=%fused_computation.42 | convolution fusion | flops 191600640 | bytes 8958033 | tf_op jit(solution)/shard_map/kvj,kij->kvi/dot_general | solution.py:60
  81.3 4.6 collective-permute-done.15
  89.1 5.8 %fusion.24 = f32[81,32,192]{2,1,0:T(8,128)S(1)} fusion(bf16[1,1,81,192,192]{4,3,2,1,0:T(8,128)(2,1)} %param.10, bf16[81,32,192]{2,1,0:T(8,128)(2,1)S(1)} %gather_fusion.3, pred[81]{0:T(512)(128)(4,1)S(1)} %compare_and_fusion), kind=kOutput, calls=%fused_computation.40 | convolution fusion | flops 191600640 | bytes 8958033 | tf_op jit(solution)/shard_map/kvj,kij->kvi/dot_general | solution.py:60
  104.5 4.8 %collective-permute-done.19 = bf16[3,1,3,32,192]{4,2,3,1,0:T(4,128)(2,1)S(1)} collective-permute-done((bf16[3,1,3,32,192]{4,2,3,1,0:T(4,128)(2,1)S(1)}, bf16[3,1,3,32,192]{4,2,3,1,0:T(4,128)(2,1)S(1)}, u32[]{:S(2)}, u32[]{:S(2)}) %collective-permute-start.19) | collective-permute-done | bytes 110624 | tf_op jit(solution)/shard_map/ppermute | solution.py:23
  112.7 5.8 %fusion.22 = f32[81,32,192]{2,1,0:T(8,128)S(1)} fusion(bf16[1,1,81,192,192]{4,3,2,1,0:T(8,128)(2,1)} %param.10, bf16[81,32,192]{2,1,0:T(8,128)(2,1)S(1)} %gather_fusion.4, pred[81]{0:T(512)(128)(4,1)S(1)} %compare_and_fusion), kind=kOutput, calls=%fused_computation.38 | convolution fusion | flops 191600640 | bytes 8958033 | tf_op jit(solution)/shard_map/kvj,kij->kvi/dot_general | solution.py:60
  127.5 4.6 collective-permute-done.23
  135.3 5.8 %fusion.20 = f32[81,32,192]{2,1,0:T(8,128)S(1)} fusion(bf16[1,1,81,192,192]{4,3,2,1,0:T(8,128)(2,1)} %param.10, bf16[81,32,192]{2,1,0:T(8,128)(2,1)S(1)} %gather_fusion.5, pred[81]{0:T(512)(128)(4,1)S(1)} %compare_and_fusion), kind=kOutput, calls=%fused_computation.36 | convolution fusion | flops 191600640 | bytes 8958033 | tf_op jit(solution)/shard_map/kvj,kij->kvi/dot_general | solution.py:60
  150.9 4.6 collective-permute-done.27
  159.1 5.8 %fusion.18 = f32[81,32,192]{2,1,0:T(8,128)S(1)} fusion(bf16[1,1,81,192,192]{4,3,2,1,0:T(8,128)(2,1)} %param.10, bf16[81,32,192]{2,1,0:T(8,128)(2,1)S(1)} %gather_fusion.6, pred[81]{0:T(512)(128)(4,1)S(1)} %compare_and_fusion), kind=kOutput, calls=%fused_computation.34 | convolution fusion | flops 191600640 | bytes 8958033 | tf_op jit(solution)/shard_map/kvj,kij->kvi/dot_general | solution.py:60
  182.4 5.8 %fusion.16 = f32[81,32,192]{2,1,0:T(8,128)S(1)} fusion(bf16[1,1,81,192,192]{4,3,2,1,0:T(8,128)(2,1)} %param.10, bf16[81,32,192]{2,1,0:T(8,128)(2,1)S(1)} %gather_fusion.7, pred[81]{0:T(512)(128)(4,1)S(1)} %compare_and_fusion), kind=kOutput, calls=%fused_computation.32 | convolution fusion | flops 191600640 | bytes 8958033 | tf_op jit(solution)/shard_map/kvj,kij->kvi/dot_general | solution.py:60
  191.0 27.5 %psum.28 = f32[32,32]{0,1:T(8,128)S(1)} all-reduce(f32[32,32]{0,1:T(8,128)S(1)} %convolution_bitcast_fusion.3), channel_id=1, replica_groups=mesh['gx'=4,'gy'=8] {'gy'}, use_global_device_ids=true, to_apply=%region_0.0 | all-reduce | flops 1024 | bytes 8192 | tf_op jit(solution)/shard_map/psum | solution.py:35
  218.5 14.4 %psum.29 = f32[32,32]{0,1:T(8,128)S(1)} all-reduce(f32[32,32]{0,1:T(8,128)S(1)} %psum.28), channel_id=1, replica_groups=mesh['gx'=4,'gy'=8] {'gx'}, use_global_device_ids=true, to_apply=%region_1.3 | all-reduce | flops 1024 | bytes 8192 | tf_op jit(solution)/shard_map/psum | solution.py:35
  253.9 5.8 %fusion.14 = f32[81,32,192]{2,1,0:T(8,128)S(1)} fusion(bf16[1,1,81,192,192]{4,3,2,1,0:T(8,128)(2,1)} %param.10, bf16[81,32,192]{2,1,0:T(8,128)(2,1)S(1)} %gather_fusion.8, pred[81]{0:T(512)(128)(4,1)S(1)} %compare_and_fusion), kind=kOutput, calls=%fused_computation.30 | convolution fusion | flops 191600640 | bytes 8958033 | tf_op jit(solution)/shard_map/kvj,kij->kvi/dot_general | solution.py:60
  274.8 5.8 %fusion.12 = f32[81,32,192]{2,1,0:T(8,128)S(1)} fusion(bf16[1,1,81,192,192]{4,3,2,1,0:T(8,128)(2,1)} %param.10, bf16[81,32,192]{2,1,0:T(8,128)(2,1)S(1)} %gather_fusion.9, pred[81]{0:T(512)(128)(4,1)S(1)} %compare_and_fusion), kind=kOutput, calls=%fused_computation.28 | convolution fusion | flops 191600640 | bytes 8958033 | tf_op jit(solution)/shard_map/kvj,kij->kvi/dot_general | solution.py:60
  296.9 5.8 %fusion.10 = f32[81,32,192]{2,1,0:T(8,128)S(1)} fusion(bf16[1,1,81,192,192]{4,3,2,1,0:T(8,128)(2,1)} %param.10, bf16[81,32,192]{2,1,0:T(8,128)(2,1)S(1)} %gather_fusion.10, pred[81]{0:T(512)(128)(4,1)S(1)} %compare_and_fusion), kind=kOutput, calls=%fused_computation.26 | convolution fusion | flops 191600640 | bytes 8958033 | tf_op jit(solution)/shard_map/kvj,kij->kvi/dot_general | solution.py:60
  318.2 5.8 %fusion.8 = f32[81,32,192]{2,1,0:T(8,128)S(1)} fusion(bf16[1,1,81,192,192]{4,3,2,1,0:T(8,128)(2,1)} %param.10, bf16[81,32,192]{2,1,0:T(8,128)(2,1)S(1)} %gather_fusion.11, pred[81]{0:T(512)(128)(4,1)S(1)} %compare_and_fusion), kind=kOutput, calls=%fused_computation.24 | convolution fusion | flops 191600640 | bytes 8958033 | tf_op jit(solution)/shard_map/kvj,kij->kvi/dot_general | solution.py:60
  340.8 5.8 %fusion.6 = f32[81,32,192]{2,1,0:T(8,128)S(1)} fusion(bf16[1,1,81,192,192]{4,3,2,1,0:T(8,128)(2,1)} %param.10, bf16[81,32,192]{2,1,0:T(8,128)(2,1)S(1)} %gather_fusion.12, pred[81]{0:T(512)(128)(4,1)S(1)} %compare_and_fusion), kind=kOutput, calls=%fused_computation.22 | convolution fusion | flops 191600640 | bytes 8958033 | tf_op jit(solution)/shard_map/kvj,kij->kvi/dot_general | solution.py:60
  361.7 5.8 %fusion.4 = f32[81,32,192]{2,1,0:T(8,128)S(1)} fusion(bf16[1,1,81,192,192]{4,3,2,1,0:T(8,128)(2,1)} %param.10, bf16[81,32,192]{2,1,0:T(8,128)(2,1)S(1)} %gather_fusion.13, pred[81]{0:T(512)(128)(4,1)S(1)} %compare_and_fusion), kind=kOutput, calls=%fused_computation.20 | convolution fusion | flops 191600640 | bytes 8958033 | tf_op jit(solution)/shard_map/kvj,kij->kvi/dot_general | solution.py:60
  383.6 5.8 %fusion.2 = f32[81,32,192]{2,1,0:T(8,128)S(1)} fusion(bf16[1,1,81,192,192]{4,3,2,1,0:T(8,128)(2,1)} %param.10, bf16[81,32,192]{2,1,0:T(8,128)(2,1)S(1)} %gather_fusion.14, pred[81]{0:T(512)(128)(4,1)S(1)} %compare_and_fusion), kind=kOutput, calls=%fused_computation.18 | convolution fusion | flops 191600640 | bytes 8958033 | tf_op jit(solution)/shard_map/kvj,kij->kvi/dot_general | solution.py:60
  404.9 5.8 %fusion = f32[81,32,192]{2,1,0:T(8,128)S(1)} fusion(bf16[1,1,81,192,192]{4,3,2,1,0:T(8,128)(2,1)} %param.10, bf16[81,32,192]{2,1,0:T(8,128)(2,1)S(1)} %gather_fusion.15, pred[81]{0:T(512)(128)(4,1)S(1)} %compare_and_fusion), kind=kOutput, calls=%fused_computation.16 | convolution fusion | flops 191600640 | bytes 8958033 | tf_op jit(solution)/shard_map/kvj,kij->kvi/dot_general | solution.py:60
  413.6 27.1 %psum.30 = f32[32,32]{0,1:T(8,128)S(1)} all-reduce(f32[32,32]{0,1:T(8,128)S(1)} %convolution_bitcast_fusion.1), channel_id=1, replica_groups=mesh['gx'=4,'gy'=8] {'gy'}, use_global_device_ids=true, to_apply=%region_4.8 | all-reduce | flops 1024 | bytes 8192 | tf_op jit(solution)/shard_map/psum | solution.py:35
  440.7 15.0 %psum.31 = f32[32,32]{0,1:T(8,128)S(1)} all-reduce(f32[32,32]{0,1:T(8,128)S(1)} %psum.30), channel_id=1, replica_groups=mesh['gx'=4,'gy'=8] {'gx'}, use_global_device_ids=true, to_apply=%region_5.9 | all-reduce | flops 1024 | bytes 8192 | tf_op jit(solution)/shard_map/psum | solution.py:35
  (232 shorter events, 267.4 us)
Async XLA Ops:
  0.9 5.6 %collective-permute-start.1 = (bf16[1,1,3,32,192]{4,3,2,1,0:T(8,128)(2,1)S(1)}, bf16[1,1,3,32,192]{4,3,2,1,0:T(8,128)(2,1)S(1)}, u32[]{:S(2)}, u32[]{:S(2)}) collective-permute-start(bf16[1,1,3,32,192]{4,3,2,1,0:T(8,128)(2,1)S(1)} %convert_element_type.82), channel_id=1, source_target_pairs={{8,0},{16,8},{24,16},{0,24},{9,1},{17,9},{25,17},{1,25},{10,2},{18... | collective-permute-start | bytes 110600 | tf_op jit(solution)/shard_map/ppermute | solution.py:23
  9.8 5.4 %collective-permute-start.3 = (bf16[3,1,3,32,192]{4,3,2,1,0:T(8,128)(2,1)S(1)}, bf16[3,1,3,32,192]{4,3,2,1,0:T(8,128)(2,1)S(1)}, u32[]{:S(2)}, u32[]{:S(2)}) collective-permute-start(bf16[3,1,3,32,192]{4,3,2,1,0:T(8,128)(2,1)S(1)} %pad_maximum_fusion.23), channel_id=1, source_target_pairs={{1,0},{2,1},{3,2},{4,3},{5,4},{6,5},{7,6},{0,7},{9,8},{10,9},{11,1... | collective-permute-start | bytes 331784 | tf_op jit(solution)/shard_map/ppermute | solution.py:23
  11.5 6.7 %collective-permute-start.2 = (bf16[3,1,3,32,192]{4,3,2,1,0:T(8,128)(2,1)S(1)}, bf16[3,1,3,32,192]{4,3,2,1,0:T(8,128)(2,1)S(1)}, u32[]{:S(2)}, u32[]{:S(2)}) collective-permute-start(bf16[3,1,3,32,192]{4,3,2,1,0:T(8,128)(2,1)S(1)} %pad_maximum_fusion.23), channel_id=1, source_target_pairs={{0,1},{1,2},{2,3},{3,4},{4,5},{5,6},{6,7},{7,0},{8,9},{9,10},{10,1... | collective-permute-start | bytes 331784 | tf_op jit(solution)/shard_map/ppermute | solution.py:21
  27.5 5.2 %collective-permute-start.4 = (bf16[1,1,3,32,192]{4,2,3,1,0:T(4,128)(2,1)S(1)}, bf16[1,1,3,32,192]{4,2,3,1,0:T(4,128)(2,1)S(1)}, u32[]{:S(2)}, u32[]{:S(2)}) collective-permute-start(bf16[1,1,3,32,192]{4,2,3,1,0:T(4,128)(2,1)S(1)} %get-tuple-element.18), channel_id=1, source_target_pairs={{0,8},{8,16},{16,24},{24,0},{1,9},{9,17},{17,25},{25,1},{2,10},{10... | collective-permute-start | bytes 110600 | tf_op jit(solution)/shard_map/ppermute | solution.py:21
  32.9 7.3 %collective-permute-start.6 = (bf16[3,1,3,32,192]{4,2,3,1,0:T(4,128)(2,1)S(1)}, bf16[3,1,3,32,192]{4,2,3,1,0:T(4,128)(2,1)S(1)}, u32[]{:S(2)}, u32[]{:S(2)}) collective-permute-start(bf16[3,1,3,32,192]{4,2,3,1,0:T(4,128)(2,1)S(1)} %pad_maximum_fusion.16), channel_id=1, source_target_pairs={{0,1},{1,2},{2,3},{3,4},{4,5},{5,6},{6,7},{7,0},{8,9},{9,10},{10,1... | collective-permute-start | bytes 331784 | tf_op jit(solution)/shard_map/ppermute | solution.py:21
  56.3 5.3 %collective-permute-start.11 = (bf16[3,1,3,32,192]{4,2,3,1,0:T(4,128)(2,1)S(1)}, bf16[3,1,3,32,192]{4,2,3,1,0:T(4,128)(2,1)S(1)}, u32[]{:S(2)}, u32[]{:S(2)}) collective-permute-start(bf16[3,1,3,32,192]{4,2,3,1,0:T(4,128)(2,1)S(1)} %pad_maximum_fusion.17), channel_id=1, source_target_pairs={{1,0},{2,1},{3,2},{4,3},{5,4},{6,5},{7,6},{0,7},{9,8},{10,9},{11,1... | collective-permute-start | bytes 331784 | tf_op jit(solution)/shard_map/ppermute | solution.py:23
  57.7 7.0 %collective-permute-start.10 = (bf16[3,1,3,32,192]{4,2,3,1,0:T(4,128)(2,1)S(1)}, bf16[3,1,3,32,192]{4,2,3,1,0:T(4,128)(2,1)S(1)}, u32[]{:S(2)}, u32[]{:S(2)}) collective-permute-start(bf16[3,1,3,32,192]{4,2,3,1,0:T(4,128)(2,1)S(1)} %pad_maximum_fusion.17), channel_id=1, source_target_pairs={{0,1},{1,2},{2,3},{3,4},{4,5},{5,6},{6,7},{7,0},{8,9},{9,10},{10,1... | collective-permute-start | bytes 331784 | tf_op jit(solution)/shard_map/ppermute | solution.py:21
  80.8 5.2 %collective-permute-start.15 = (bf16[3,1,3,32,192]{4,2,3,1,0:T(4,128)(2,1)S(1)}, bf16[3,1,3,32,192]{4,2,3,1,0:T(4,128)(2,1)S(1)}, u32[]{:S(2)}, u32[]{:S(2)}) collective-permute-start(bf16[3,1,3,32,192]{4,2,3,1,0:T(4,128)(2,1)S(1)} %pad_maximum_fusion.18), channel_id=1, source_target_pairs={{1,0},{2,1},{3,2},{4,3},{5,4},{6,5},{7,6},{0,7},{9,8},{10,9},{11,1... | collective-permute-start | bytes 331784 | tf_op jit(solution)/shard_map/ppermute | solution.py:23
  80.8 6.9 %collective-permute-start.14 = (bf16[3,1,3,32,192]{4,2,3,1,0:T(4,128)(2,1)S(1)}, bf16[3,1,3,32,192]{4,2,3,1,0:T(4,128)(2,1)S(1)}, u32[]{:S(2)}, u32[]{:S(2)}) collective-permute-start(bf16[3,1,3,32,192]{4,2,3,1,0:T(4,128)(2,1)S(1)} %pad_maximum_fusion.18), channel_id=1, source_target_pairs={{0,1},{1,2},{2,3},{3,4},{4,5},{5,6},{6,7},{7,0},{8,9},{9,10},{10,1... | collective-permute-start | bytes 331784 | tf_op jit(solution)/shard_map/ppermute | solution.py:21
  103.8 5.5 %collective-permute-start.19 = (bf16[3,1,3,32,192]{4,2,3,1,0:T(4,128)(2,1)S(1)}, bf16[3,1,3,32,192]{4,2,3,1,0:T(4,128)(2,1)S(1)}, u32[]{:S(2)}, u32[]{:S(2)}) collective-permute-start(bf16[3,1,3,32,192]{4,2,3,1,0:T(4,128)(2,1)S(1)} %pad_maximum_fusion.19), channel_id=1, source_target_pairs={{1,0},{2,1},{3,2},{4,3},{5,4},{6,5},{7,6},{0,7},{9,8},{10,9},{11,1... | collective-permute-start | bytes 331784 | tf_op jit(solution)/shard_map/ppermute | solution.py:23
  104.2 7.1 %collective-permute-start.18 = (bf16[3,1,3,32,192]{4,2,3,1,0:T(4,128)(2,1)S(1)}, bf16[3,1,3,32,192]{4,2,3,1,0:T(4,128)(2,1)S(1)}, u32[]{:S(2)}, u32[]{:S(2)}) collective-permute-start(bf16[3,1,3,32,192]{4,2,3,1,0:T(4,128)(2,1)S(1)} %pad_maximum_fusion.19), channel_id=1, source_target_pairs={{0,1},{1,2},{2,3},{3,4},{4,5},{5,6},{6,7},{7,0},{8,9},{9,10},{10,1... | collective-permute-start | bytes 331784 | tf_op jit(solution)/shard_map/ppermute | solution.py:21
  127.0 5.2 %collective-permute-start.23 = (bf16[3,1,3,32,192]{4,2,3,1,0:T(4,128)(2,1)S(1)}, bf16[3,1,3,32,192]{4,2,3,1,0:T(4,128)(2,1)S(1)}, u32[]{:S(2)}, u32[]{:S(2)}) collective-permute-start(bf16[3,1,3,32,192]{4,2,3,1,0:T(4,128)(2,1)S(1)} %pad_maximum_fusion.20), channel_id=1, source_target_pairs={{1,0},{2,1},{3,2},{4,3},{5,4},{6,5},{7,6},{0,7},{9,8},{10,9},{11,1... | collective-permute-start | bytes 331784 | tf_op jit(solution)/shard_map/ppermute | solution.py:23
  127.0 6.9 %collective-permute-start.22 = (bf16[3,1,3,32,192]{4,2,3,1,0:T(4,128)(2,1)S(1)}, bf16[3,1,3,32,192]{4,2,3,1,0:T(4,128)(2,1)S(1)}, u32[]{:S(2)}, u32[]{:S(2)}) collective-permute-start(bf16[3,1,3,32,192]{4,2,3,1,0:T(4,128)(2,1)S(1)} %pad_maximum_fusion.20), channel_id=1, source_target_pairs={{0,1},{1,2},{2,3},{3,4},{4,5},{5,6},{6,7},{7,0},{8,9},{9,10},{10,1... | collective-permute-start | bytes 331784 | tf_op jit(solution)/shard_map/ppermute | solution.py:21
  150.0 5.6 %collective-permute-start.27 = (bf16[3,1,3,32,192]{4,2,3,1,0:T(4,128)(2,1)S(1)}, bf16[3,1,3,32,192]{4,2,3,1,0:T(4,128)(2,1)S(1)}, u32[]{:S(2)}, u32[]{:S(2)}) collective-permute-start(bf16[3,1,3,32,192]{4,2,3,1,0:T(4,128)(2,1)S(1)} %pad_maximum_fusion.21), channel_id=1, source_target_pairs={{1,0},{2,1},{3,2},{4,3},{5,4},{6,5},{7,6},{0,7},{9,8},{10,9},{11,1... | collective-permute-start | bytes 331784 | tf_op jit(solution)/shard_map/ppermute | solution.py:23
  150.5 7.3 %collective-permute-start.26 = (bf16[3,1,3,32,192]{4,2,3,1,0:T(4,128)(2,1)S(1)}, bf16[3,1,3,32,192]{4,2,3,1,0:T(4,128)(2,1)S(1)}, u32[]{:S(2)}, u32[]{:S(2)}) collective-permute-start(bf16[3,1,3,32,192]{4,2,3,1,0:T(4,128)(2,1)S(1)} %pad_maximum_fusion.21), channel_id=1, source_target_pairs={{0,1},{1,2},{2,3},{3,4},{4,5},{5,6},{6,7},{7,0},{8,9},{9,10},{10,1... | collective-permute-start | bytes 331784 | tf_op jit(solution)/shard_map/ppermute | solution.py:21
  174.2 6.9 %collective-permute-start.30 = (bf16[3,1,3,32,192]{4,2,3,1,0:T(4,128)(2,1)S(1)}, bf16[3,1,3,32,192]{4,2,3,1,0:T(4,128)(2,1)S(1)}, u32[]{:S(2)}, u32[]{:S(2)}) collective-permute-start(bf16[3,1,3,32,192]{4,2,3,1,0:T(4,128)(2,1)S(1)} %pad_maximum_fusion.22), channel_id=1, source_target_pairs={{0,1},{1,2},{2,3},{3,4},{4,5},{5,6},{6,7},{7,0},{8,9},{9,10},{10,1... | collective-permute-start | bytes 331784 | tf_op jit(solution)/shard_map/ppermute | solution.py:21
  246.7 6.4 %collective-permute-start.34 = (bf16[3,1,3,32,192]{4,3,2,1,0:T(8,128)(2,1)S(1)}, bf16[3,1,3,32,192]{4,3,2,1,0:T(8,128)(2,1)S(1)}, u32[]{:S(2)}, u32[]{:S(2)}) collective-permute-start(bf16[3,1,3,32,192]{4,3,2,1,0:T(8,128)(2,1)S(1)} %pad_maximum_fusion.24), channel_id=1, source_target_pairs={{0,1},{1,2},{2,3},{3,4},{4,5},{5,6},{6,7},{7,0},{8,9},{9,10},{10,1... | collective-permute-start | bytes 331784 | tf_op jit(solution)/shard_map/ppermute | solution.py:21
  267.7 6.4 %collective-permute-start.38 = (bf16[3,1,3,32,192]{4,3,2,1,0:T(8,128)(2,1)S(1)}, bf16[3,1,3,32,192]{4,3,2,1,0:T(8,128)(2,1)S(1)}, u32[]{:S(2)}, u32[]{:S(2)}) collective-permute-start(bf16[3,1,3,32,192]{4,3,2,1,0:T(8,128)(2,1)S(1)} %pad_maximum_fusion.25), channel_id=1, source_target_pairs={{0,1},{1,2},{2,3},{3,4},{4,5},{5,6},{6,7},{7,0},{8,9},{9,10},{10,1... | collective-permute-start | bytes 331784 | tf_op jit(solution)/shard_map/ppermute | solution.py:21
  289.5 6.6 %collective-permute-start.42 = (bf16[3,1,3,32,192]{4,3,2,1,0:T(8,128)(2,1)S(1)}, bf16[3,1,3,32,192]{4,3,2,1,0:T(8,128)(2,1)S(1)}, u32[]{:S(2)}, u32[]{:S(2)}) collective-permute-start(bf16[3,1,3,32,192]{4,3,2,1,0:T(8,128)(2,1)S(1)} %pad_maximum_fusion.26), channel_id=1, source_target_pairs={{0,1},{1,2},{2,3},{3,4},{4,5},{5,6},{6,7},{7,0},{8,9},{9,10},{10,1... | collective-permute-start | bytes 331784 | tf_op jit(solution)/shard_map/ppermute | solution.py:21
  311.1 6.4 %collective-permute-start.46 = (bf16[3,1,3,32,192]{4,3,2,1,0:T(8,128)(2,1)S(1)}, bf16[3,1,3,32,192]{4,3,2,1,0:T(8,128)(2,1)S(1)}, u32[]{:S(2)}, u32[]{:S(2)}) collective-permute-start(bf16[3,1,3,32,192]{4,3,2,1,0:T(8,128)(2,1)S(1)} %pad_maximum_fusion.27), channel_id=1, source_target_pairs={{0,1},{1,2},{2,3},{3,4},{4,5},{5,6},{6,7},{7,0},{8,9},{9,10},{10,1... | collective-permute-start | bytes 331784 | tf_op jit(solution)/shard_map/ppermute | solution.py:21
  333.2 6.8 %collective-permute-start.50 = (bf16[3,1,3,32,192]{4,3,2,1,0:T(8,128)(2,1)S(1)}, bf16[3,1,3,32,192]{4,3,2,1,0:T(8,128)(2,1)S(1)}, u32[]{:S(2)}, u32[]{:S(2)}) collective-permute-start(bf16[3,1,3,32,192]{4,3,2,1,0:T(8,128)(2,1)S(1)} %pad_maximum_fusion.28), channel_id=1, source_target_pairs={{0,1},{1,2},{2,3},{3,4},{4,5},{5,6},{6,7},{7,0},{8,9},{9,10},{10,1... | collective-permute-start | bytes 331784 | tf_op jit(solution)/shard_map/ppermute | solution.py:21
  354.5 6.4 %collective-permute-start.54 = (bf16[3,1,3,32,192]{4,3,2,1,0:T(8,128)(2,1)S(1)}, bf16[3,1,3,32,192]{4,3,2,1,0:T(8,128)(2,1)S(1)}, u32[]{:S(2)}, u32[]{:S(2)}) collective-permute-start(bf16[3,1,3,32,192]{4,3,2,1,0:T(8,128)(2,1)S(1)} %pad_maximum_fusion.29), channel_id=1, source_target_pairs={{0,1},{1,2},{2,3},{3,4},{4,5},{5,6},{6,7},{7,0},{8,9},{9,10},{10,1... | collective-permute-start | bytes 331784 | tf_op jit(solution)/shard_map/ppermute | solution.py:21
  376.2 6.6 %collective-permute-start.58 = (bf16[3,1,3,32,192]{4,3,2,1,0:T(8,128)(2,1)S(1)}, bf16[3,1,3,32,192]{4,3,2,1,0:T(8,128)(2,1)S(1)}, u32[]{:S(2)}, u32[]{:S(2)}) collective-permute-start(bf16[3,1,3,32,192]{4,3,2,1,0:T(8,128)(2,1)S(1)} %pad_maximum_fusion.30), channel_id=1, source_target_pairs={{0,1},{1,2},{2,3},{3,4},{4,5},{5,6},{6,7},{7,0},{8,9},{9,10},{10,1... | collective-permute-start | bytes 331784 | tf_op jit(solution)/shard_map/ppermute | solution.py:21
  397.8 6.4 %collective-permute-start.62 = (bf16[3,1,3,32,192]{4,3,2,1,0:T(8,128)(2,1)S(1)}, bf16[3,1,3,32,192]{4,3,2,1,0:T(8,128)(2,1)S(1)}, u32[]{:S(2)}, u32[]{:S(2)}) collective-permute-start(bf16[3,1,3,32,192]{4,3,2,1,0:T(8,128)(2,1)S(1)} %pad_maximum_fusion.31), channel_id=1, source_target_pairs={{0,1},{1,2},{2,3},{3,4},{4,5},{5,6},{6,7},{7,0},{8,9},{9,10},{10,1... | collective-permute-start | bytes 331784 | tf_op jit(solution)/shard_map/ppermute | solution.py:21
  (42 other events, 194.6 us)
